TPU v7x, 32 devices: a whole 2x2x4 slice. The times are simulated.
32 devices in a mesh: dp: 2 (over x), mp: 16 (over z, y, core).
Axes of the slice: x: 2, y: 2, z: 4, core: 2. Of those that a mesh axis runs over, the one named last changes fastest.
Arguments:
- node_features: bfloat16 [512, 6144], P('mp', 'dp'), may hold values from -6 to 6
- weights_one: bfloat16 [1024, 512], replicated, may hold values from -0.25 to 0.25
- weights_two: bfloat16 [1024, 512], replicated, may hold values from -0.25 to 0.25
- neighbor_owner: int32 [6144, 8], P('dp'), may hold values from 0 to 15, all different within a row; in each aligned block of 192 rows (0 to 191, 192 to 383, ...) at most 144 rows name the same one
- neighbor_row: int32 [6144, 8], P('dp'), may hold values from 0 to 191
- neighbor_count: int32 [6144], P('dp'), may hold values from 4 to 8
- cotangent: bfloat16 [6144, 512], P(('dp', 'mp')), may hold values from -0.076171875 to 0.076171875
Outputs:
- node_output: bfloat16 [6144, 512], P(('dp', 'mp'))
- weight_grads: float32 [2048, 512], P(('dp', 'mp'))
Inputs may be any that keep to these rules, and one draw needn't show every extreme that they name: `neighbor_owner`: each row names 8 different owners; among the rows of one device (aligned blocks of 192 rows) no owner is named more than 144 times, and in some block one owner exactly 144 times. Slots k >= neighbor_count[r] are padding and carry no edge.
All inputs are finite; a program needn't handle non-finite values.
Results may differ from a plain program's by a relative error of at most 0.0052.
Values may be sent and summed in bfloat16 or wider, within the bound.
No kernel may reach another device: no remote copies, remote signals or barrier semaphores. Data moves between devices by JAX's collectives and lax.ppermute only.
A program may use at most 64 MiB of HBM per device.

v0:
```python
import jax
import jax.numpy as jnp
from jax import lax
from jax.sharding import PartitionSpec as P


def column_mean(table, indices, live, inverse):
    total = jnp.zeros((table.shape[0], indices.shape[1]), jnp.float32)
    for slot_index in range(indices.shape[0]):
        picked = jnp.take(table, indices[slot_index], axis=1)
        kept = jnp.where(live[slot_index][None, :], picked, jnp.zeros_like(picked))
        total = total + kept.astype(jnp.float32)
    return (total * inverse[None, :]).astype(jnp.bfloat16)


def silu_slope(values):
    sigmoid = jax.nn.sigmoid(values)
    return sigmoid * (1.0 + values * (1.0 - sigmoid))


def contract(left, right, left_dim, right_dim):
    return lax.dot_general(
        left, right, (((left_dim,), (right_dim,)), ((), ())), preferred_element_type=jnp.float32
    )


def shards(
    node_features, weights_one, weights_two, neighbor_owner, neighbor_row, neighbor_count, cotangent
):
    devices = lax.axis_size("mp")
    own_index = lax.axis_index("mp")
    node_dev = cotangent.shape[0]
    all_nodes = neighbor_owner.shape[0]
    fanout = neighbor_owner.shape[1]
    feat_width = weights_one.shape[0] // 2
    hidden = weights_one.shape[1]
    capacity = 3 * node_dev * fanout // (2 * devices)
    live = lax.broadcasted_iota(jnp.int32, (all_nodes, fanout), 1) < neighbor_count[:, None]
    inverse_all = 1.0 / neighbor_count.astype(jnp.float32)
    owner_ids = lax.broadcasted_iota(jnp.int32, (devices, 1, 1), 0)
    match = (neighbor_owner[None, :, :] == owner_ids) & live[None, :, :]
    rowsel = jnp.max(jnp.where(match, neighbor_row[None, :, :], -1), axis=2)
    has = rowsel >= 0
    with jax.named_scope("layer_one_mean"):
        if all_nodes * all_nodes <= 4096 * 4096:
            row_ids = lax.broadcasted_iota(jnp.int32, (1, node_dev, 1), 1)
            adjacency = (rowsel[:, None, :] == row_ids).astype(jnp.bfloat16)
            adjacency = adjacency.reshape(devices * node_dev, all_nodes)
            summed = contract(node_features, adjacency, 1, 0)
            agg_one_cols = (summed * inverse_all[None, :]).astype(jnp.bfloat16)
        else:
            owner_slots = neighbor_owner.T
            global_ids = owner_slots * node_dev + neighbor_row.T
            agg_one_cols = column_mean(node_features, global_ids, live.T, inverse_all)
    own_feats, own_agg_one = (
        lax.all_to_all(node_features, "mp", split_axis=1, concat_axis=0, tiled=True),
        lax.all_to_all(agg_one_cols, "mp", split_axis=1, concat_axis=0, tiled=True),
    )
    pre_one = contract(weights_one[:feat_width], own_feats, 0, 0) + contract(
        weights_one[feat_width:], own_agg_one, 0, 0
    )
    hidden_one = jax.nn.silu(pre_one).astype(jnp.bfloat16)
    with jax.named_scope("slot_tables"):
        blocks = has.reshape(devices * devices, node_dev).astype(jnp.bfloat16)
        before = (
            lax.broadcasted_iota(jnp.int32, (node_dev, node_dev), 0)
            < lax.broadcasted_iota(jnp.int32, (node_dev, node_dev), 1)
        ).astype(jnp.bfloat16)
        ranks = contract(blocks, before, 1, 0).astype(jnp.int32).reshape(devices, devices, node_dev)
        has_blocks = has.reshape(devices, devices, node_dev)
        rows_blocks = rowsel.reshape(devices, devices, node_dev)
        cap_ids = lax.broadcasted_iota(jnp.int32, (1, capacity, 1), 1)
        own_rank = lax.dynamic_index_in_dim(ranks, own_index, 1, keepdims=False)
        own_has = lax.dynamic_index_in_dim(has_blocks, own_index, 1, keepdims=False)
        gathered = ((own_rank[:, None, :] == cap_ids) & own_has[:, None, :]).astype(jnp.bfloat16)
        gathered = gathered.reshape(devices * capacity, node_dev)
        req_rank = lax.dynamic_index_in_dim(ranks, own_index, 0, keepdims=False)
        req_has = lax.dynamic_index_in_dim(has_blocks, own_index, 0, keepdims=False)
        req_rows = lax.dynamic_index_in_dim(rows_blocks, own_index, 0, keepdims=False)
        pick = ((req_rank[:, None, :] == cap_ids) & req_has[:, None, :]).astype(jnp.bfloat16)
        row_ids = lax.broadcasted_iota(jnp.int32, (1, 1, node_dev), 2)
        which = (req_rows[:, :, None] == row_ids).astype(jnp.bfloat16)
        asked = lax.dot_general(
            pick, which, (((2,), (1,)), ((0,), (0,))), preferred_element_type=jnp.float32
        )
        asked = asked.astype(jnp.bfloat16).reshape(devices * capacity, node_dev)
    own_inverse = lax.dynamic_slice_in_dim(inverse_all, own_index * node_dev, node_dev, 0)
    outgoing = contract(hidden_one, asked, 1, 1).astype(jnp.bfloat16)
    incoming = lax.all_to_all(outgoing, "mp", split_axis=1, concat_axis=1, tiled=True)
    total = contract(incoming, gathered, 1, 0)
    agg_two = (total * own_inverse[None, :]).astype(jnp.bfloat16)
    self_two = weights_two[:hidden]
    neigh_two = weights_two[hidden:]
    node_output = (
        contract(hidden_one, self_two, 0, 0) + contract(agg_two, neigh_two, 0, 0)
    ).astype(jnp.bfloat16)
    down_self = contract(self_two, cotangent, 1, 1)
    down_neigh = (contract(neigh_two, cotangent, 1, 1) * own_inverse[None, :]).astype(jnp.bfloat16)
    outgoing_grad = contract(down_neigh, gathered, 1, 1).astype(jnp.bfloat16)
    incoming_grad = lax.all_to_all(outgoing_grad, "mp", split_axis=1, concat_axis=1, tiled=True)
    neighbor_sum = contract(incoming_grad, asked, 1, 0)
    grad_hidden = down_self + neighbor_sum
    grad_pre = (grad_hidden * silu_slope(pre_one)).astype(jnp.bfloat16)
    terms = jnp.concatenate(
        [
            contract(own_feats, grad_pre, 1, 1),
            contract(own_agg_one, grad_pre, 1, 1),
            contract(hidden_one, cotangent, 1, 0),
            contract(agg_two, cotangent, 1, 0),
        ],
        axis=0,
    )
    weight_grads = lax.psum_scatter(terms, ("dp", "mp"), scatter_dimension=0, tiled=True)
    return (node_output, weight_grads)


def solution(mesh):
    in_specs = (
        P("mp", "dp"),
        P(),
        P(),
        P("dp", None),
        P("dp", None),
        P("dp"),
        P(("dp", "mp"), None),
    )
    out_specs = (P(("dp", "mp"), None), P(("dp", "mp"), None))
    return jax.shard_map(shards, mesh=mesh, in_specs=in_specs, out_specs=out_specs, check_vma=False)
```

profile of v0, /device:TPU:0, one launch (start us, length us, event | category | flops | bytes accessed | tf_op | source)
XLA Modules:
  0.0 325.1 jit_solution(16609977738096543799)
XLA Ops:
  7.2 1.3 all_to_all.40
  8.5 0.8 copy.27
  9.3 7.4 %all-to-all-start = ((bf16[32,16,192]{2,0,1:T(8,128)(2,1)}), bf16[32,16,192]{2,0,1:T(8,128)(2,1)S(1)}, u32[]{:S(2)}, u32[]{:S(2)}) async-start(bf16[32,16,192]{2,0,1:T(8,128)(2,1)} %copy.27), calls=%async_computation | async-start | bytes 524288 | tf_op jit(solution)/shard_map/all_to_all | solution.py:56
  16.7 0.7 iota_compare_fusion.9
  17.4 0.7 convert_divide_fusion
  18.2 1.8 select_reduce_fusion
  20.0 9.7 %bitcast_compare_fusion = pred[3072,3072]{1,0:T(32,128)(4,1)} fusion(s32[3072]{0:T(1024)S(1)} %eq.95, s32[16,3072]{1,0:T(8,128)S(1)} %select_reduce_fusion), kind=kLoop, calls=%fused_computation | loop fusion | flops 9437184 | bytes 9646080 | tf_op jit(solution)/shard_map/layer_one_mean/eq | solution.py:47
  29.9 8.5 %fusion.1 = bf16[32,3072]{1,0:T(8,128)(2,1)S(1)} fusion(pred[3072,3072]{1,0:T(32,128)(4,1)} %bitcast_compare_fusion, bf16[32,3072]{1,0:T(8,128)(2,1)S(1)} %copy-done.7, f32[3072]{0:T(1024)S(1)} %convert_divide_fusion), kind=kOutput, calls=%fused_computation.6 | convolution fusion | flops 604176384 | bytes 9842688 | tf_op jit(solution)/shard_map/layer_one_mean/dot_general | solution.py:22
  38.4 0.4 convolution_convert_fusion.2
  39.3 0.8 copy.28
  40.4 6.1 %all-to-all-start.1 = ((bf16[32,16,192]{2,0,1:T(8,128)(2,1)}), bf16[32,16,192]{2,0,1:T(8,128)(2,1)}, u32[]{:S(2)}, u32[]{:S(2)}) async-start(bf16[32,16,192]{2,0,1:T(8,128)(2,1)} %copy.28), calls=%async_computation.1 | async-start | bytes 524288 | tf_op jit(solution)/shard_map/all_to_all | solution.py:57
  46.7 0.5 fusion.8
  47.2 2.2 convolution_convert_fusion
  49.4 2.5 copy.31
  51.9 4.6 %all-to-all-done.1 = bf16[32,16,192]{2,0,1:T(8,128)(2,1)} async-done(((bf16[32,16,192]{2,0,1:T(8,128)(2,1)}), bf16[32,16,192]{2,0,1:T(8,128)(2,1)}, u32[]{:S(2)}, u32[]{:S(2)}) %all-to-all-start.1) | async-done | bytes 196640 | tf_op jit(solution)/shard_map/all_to_all | solution.py:57
  56.5 3.7 %all-to-all-start.3 = ((bf16[512,16,144]{0,2,1:T(8,128)(2,1)}), bf16[512,16,144]{0,2,1:T(8,128)(2,1)S(1)}, u32[]{:S(2)}, u32[]{:S(2)}) async-start(bf16[512,16,144]{0,2,1:T(8,128)(2,1)} %bitcast.16), calls=%async_computation.3 | async-start | bytes 4718592 | tf_op jit(solution)/shard_map/all_to_all | solution.py:100
  60.3 0.8 dynamic-slice_bitcast_fusion
  61.1 1.3 fusion.11
  62.8 1.3 fusion.18
  64.1 2.4 convolution_convert_fusion.1
  66.5 4.3 %copy.30 = bf16[512,2304]{0,1:T(8,128)(2,1)} copy(bf16[512,2304]{1,0:T(8,128)(2,1)} %convolution_convert_fusion.1) | data formatting | bytes 4718592 | tf_op jit(solution)/shard_map/convert_element_type | solution.py:88
  70.8 35.1 %all-to-all-done.3 = bf16[512,16,144]{0,2,1:T(8,128)(2,1)S(1)} async-done(((bf16[512,16,144]{0,2,1:T(8,128)(2,1)}), bf16[512,16,144]{0,2,1:T(8,128)(2,1)S(1)}, u32[]{:S(2)}, u32[]{:S(2)}) %all-to-all-start.3) | async-done | bytes 2359328 | tf_op jit(solution)/shard_map/all_to_all | solution.py:100
  105.9 12.3 %all-to-all-start.2 = ((bf16[512,16,144]{0,2,1:T(8,128)(2,1)}), bf16[512,16,144]{0,2,1:T(8,128)(2,1)}, u32[]{:S(2)}, u32[]{:S(2)}) async-start(bf16[512,16,144]{0,2,1:T(8,128)(2,1)} %bitcast.12), calls=%async_computation.2 | async-start | bytes 4718592 | tf_op jit(solution)/shard_map/all_to_all | solution.py:89
  118.2 1.4 fusion.42
  119.6 2.0 convolution_bitcast_fusion.1
  122.0 1.2 fusion.43
  123.5 40.4 %all-to-all-done.2 = bf16[512,16,144]{0,2,1:T(8,128)(2,1)} async-done(((bf16[512,16,144]{0,2,1:T(8,128)(2,1)}), bf16[512,16,144]{0,2,1:T(8,128)(2,1)}, u32[]{:S(2)}, u32[]{:S(2)}) %all-to-all-start.2) | async-done | bytes 2359328 | tf_op jit(solution)/shard_map/all_to_all | solution.py:89
  163.9 2.6 fusion.26
  166.9 2.4 pad_maximum_fusion
  169.3 1.2 copy-done.4
  170.8 1.0 fusion.30
  171.7 146.5 %reduce-scatter.2.cloned.1.call-done = f32[64,512]{1,0:T(8,128)} async-done(((f32[2048,512]{1,0:T(8,128)}), f32[64,512]{1,0:T(8,128)}) %reduce-scatter.2.cloned.1.call-update) | async-done | bytes 131088 | tf_op jit(solution)/shard_map/reduce_scatter | solution.py:113
  (41 shorter events, 2.8 us)
Async XLA Ops:
  7.2 40.0 %copy-start = (bf16[192,512]{1,0:T(8,128)(2,1)S(1)}, bf16[192,512]{1,0:T(8,128)(2,1)}, u32[]{:S(2)}) copy-start(bf16[192,512]{1,0:T(8,128)(2,1)} %param.13) | copy-start | bytes 589828
  9.3 31.1 %all-to-all-start = ((bf16[32,16,192]{2,0,1:T(8,128)(2,1)}), bf16[32,16,192]{2,0,1:T(8,128)(2,1)S(1)}, u32[]{:S(2)}, u32[]{:S(2)}) async-start(bf16[32,16,192]{2,0,1:T(8,128)(2,1)} %copy.27), calls=%async_computation | async-start | bytes 524288 | tf_op jit(solution)/shard_map/all_to_all | solution.py:56
  20.0 9.9 %copy-start.7 = (bf16[32,3072]{1,0:T(8,128)(2,1)S(1)}, bf16[32,3072]{1,0:T(8,128)(2,1)}, u32[]{:S(2)}) copy-start(bf16[32,3072]{1,0:T(8,128)(2,1)} %param.7) | copy-start | bytes 589828
  39.0 7.7 %copy-start.1 = (s32[16,16,192]{2,1,0:T(8,128)}, s32[16,16,192]{2,1,0:T(8,128)S(1)}, u32[]{:S(2)}) copy-start(s32[16,16,192]{2,1,0:T(8,128)S(1)} %reduce_max.12) | copy-start | bytes 589828
  40.2 6.4 %copy-start.6 = (s32[256,192]{1,0:T(8,128)}, s32[256,192]{1,0:T(8,128)S(1)}, u32[]{:S(2)}) copy-start(s32[256,192]{1,0:T(8,128)S(1)} %copy.29) | copy-start | bytes 589828
  40.4 16.2 %all-to-all-start.1 = ((bf16[32,16,192]{2,0,1:T(8,128)(2,1)}), bf16[32,16,192]{2,0,1:T(8,128)(2,1)}, u32[]{:S(2)}, u32[]{:S(2)}) async-start(bf16[32,16,192]{2,0,1:T(8,128)(2,1)} %copy.28), calls=%async_computation.1 | async-start | bytes 524288 | tf_op jit(solution)/shard_map/all_to_all | solution.py:57
  56.5 49.3 %all-to-all-start.3 = ((bf16[512,16,144]{0,2,1:T(8,128)(2,1)}), bf16[512,16,144]{0,2,1:T(8,128)(2,1)S(1)}, u32[]{:S(2)}, u32[]{:S(2)}) async-start(bf16[512,16,144]{0,2,1:T(8,128)(2,1)} %bitcast.16), calls=%async_computation.3 | async-start | bytes 4718592 | tf_op jit(solution)/shard_map/all_to_all | solution.py:100
  60.3 2.2 copy-start.2
  62.5 1.7 copy-start.8
  105.9 58.0 %all-to-all-start.2 = ((bf16[512,16,144]{0,2,1:T(8,128)(2,1)}), bf16[512,16,144]{0,2,1:T(8,128)(2,1)}, u32[]{:S(2)}, u32[]{:S(2)}) async-start(bf16[512,16,144]{0,2,1:T(8,128)(2,1)} %bitcast.12), calls=%async_computation.2 | async-start | bytes 4718592 | tf_op jit(solution)/shard_map/all_to_all | solution.py:89
  118.2 200.1 %reduce-scatter.2.cloned.1.call-start = ((), (), s32[]{:S(2)}) async-start(), calls=%async_computation.5 | async-start | bytes 4325376 | tf_op jit(solution)/shard_map/reduce_scatter | solution.py:113
  119.6 2.0 copy-start.3
  163.9 3.0 copy-start.5
  169.3 1.2 copy-start.4
Sparse Core Ops, SparseCore 0:
  169.4 148.7 reduce-scatter.1
where the time goes:
time: 326 us; the launch traced here: 325 us
  waiting for transfers between devices  227 us (70%)
  starting transfers between devices  29.5 us (9%)
  matrix products  25.9 us (8%)
  other arithmetic  15.9 us (5%)
  between operations  14.4 us (4%)
  local copies, waits for them, and re-layouts  12.7 us (4%)
    reduce_scatter x1, waiting for transfers between devices, shards(): lax.psum_scatter(terms, ('dp', 'mp'), scatter_dimension=0, tiled=True)  147 us
    all_to_all x1, waiting for transfers between devices, shards(): lax.all_to_all(outgoing, 'mp', split_axis=1, concat_axis=1, tiled=True)  40.4 us
    all_to_all x1, waiting for transfers between devices, shards(): lax.all_to_all(outgoing_grad, 'mp', split_axis=1, concat_axis=1, tiled=True)  35.1 us
    dot_general x15, matrix products, contract(): lax.dot_general(left, right, (((left_dim,), (right_dim,)), ((), ())), pre...  24.6 us
    all_to_all x1, starting transfers between devices, shards(): lax.all_to_all(outgoing, 'mp', split_axis=1, concat_axis=1, tiled=True)  12.3 us
    eq x1, other arithmetic, shards(): adjacency = (rowsel[:, None, :] == row_ids).astype(jnp.bfloat16)  9.7 us
    all_to_all x1, starting transfers between devices, shards(): lax.all_to_all(node_features, 'mp', split_axis=1, concat_axis=0, tiled=True)  7.39 us
  transfers between devices with their start and end apart: 5, of which 4 were waited for; matrix products, arithmetic and copies ran while one was open for 14% of the time, Pallas kernels for 0%

commit v1 on v0

--- a/solution.py
+++ b/solution.py
@@ -2,6 +2,22 @@
 import jax.numpy as jnp
 from jax import lax
 from jax.sharding import PartitionSpec as P
+
+
+def exchange_in_pairs(shard, axis, split, join):
+    ways, here = (lax.axis_size(axis), lax.axis_index(axis))
+    width = shard.shape[split] // ways
+    shape = list(shard.shape)
+    shape[split] = width
+    height = shape[join]
+    shape[join] = height * ways
+    full = jnp.zeros(shape, shard.dtype)
+    for mask in range(ways):
+        part = lax.dynamic_slice_in_dim(shard, (here ^ mask) * width, width, axis=split)
+        if mask:
+            part = lax.ppermute(part, axis, [(d, d ^ mask) for d in range(ways)])
+        full = lax.dynamic_update_slice_in_dim(full, part, (here ^ mask) * height, axis=join)
+    return full
 
 
 def column_mean(table, indices, live, inverse):
@@ -54,7 +70,7 @@
             agg_one_cols = column_mean(node_features, global_ids, live.T, inverse_all)
     own_feats, own_agg_one = (
         lax.all_to_all(node_features, "mp", split_axis=1, concat_axis=0, tiled=True),
-        lax.all_to_all(agg_one_cols, "mp", split_axis=1, concat_axis=0, tiled=True),
+        exchange_in_pairs(agg_one_cols, "mp", 1, 0),
     )
     pre_one = contract(weights_one[:feat_width], own_feats, 0, 0) + contract(
         weights_one[feat_width:], own_agg_one, 0, 0

time: 326 us -> 321 us (0.985)
  waiting for transfers between devices: 227 us -> 209 us
  starting transfers between devices: 29.5 us -> 40.5 us
    all_to_all x1, waiting for transfers between devices: 35.1 us -> 0.01 us  [shards(): lax.all_to_all(outgoing_grad, 'mp', split_axis=1, concat_axis=1, tiled=True)]
    ppermute x0 -> x15, starting transfers between devices: none -> 22.8 us  [exchange_in_pairs(): part = lax.ppermute(part, axis, [(d, d ^ mask) for d in range(ways)])]
    ppermute x0 -> x15, waiting for transfers between devices: none -> 21.7 us  [exchange_in_pairs(): part = lax.ppermute(part, axis, [(d, d ^ mask) for d in range(ways)])]
    all_to_all x1, starting transfers between devices: 12.3 us -> 4.45 us  [shards(): lax.all_to_all(outgoing, 'mp', split_axis=1, concat_axis=1, tiled=True)]
    all_to_all x1 -> x0, starting transfers between devices: 6.07 us -> none  [shards(): lax.all_to_all(agg_one_cols, 'mp', split_axis=1, concat_axis=0, tiled=True)]
    all_to_all x1 -> x0, waiting for transfers between devices: 4.64 us -> none  [shards(): lax.all_to_all(agg_one_cols, 'mp', split_axis=1, concat_axis=0, tiled=True)]
  transfers between devices with their start and end apart: 5 -> 19, of which waited for: 4 -> 7; matrix products, arithmetic and copies ran while one was open for 14% -> 15% of each run, Pallas kernels for 0% -> 0%
where the time goes in v1:
time: 321 us; the launch traced here: 320 us
  waiting for transfers between devices  209 us (65%)
  starting transfers between devices  40.5 us (13%)
  matrix products  27.6 us (9%)
  other arithmetic  15.9 us (5%)
  between operations  14.5 us (5%)
  local copies, waits for them, and re-layouts  12.4 us (4%)
    reduce_scatter x1, waiting for transfers between devices, shards(): lax.psum_scatter(terms, ('dp', 'mp'), scatter_dimension=0, tiled=True)  147 us
    all_to_all x1, waiting for transfers between devices, shards(): lax.all_to_all(outgoing, 'mp', split_axis=1, concat_axis=1, tiled=True)  40.3 us
    dot_general x15, matrix products, contract(): lax.dot_general(left, right, (((left_dim,), (right_dim,)), ((), ())), pre...  25.5 us
    ppermute x15, starting transfers between devices, exchange_in_pairs(): part = lax.ppermute(part, axis, [(d, d ^ mask) for d in range(ways)])  22.8 us
    ppermute x15, waiting for transfers between devices, exchange_in_pairs(): part = lax.ppermute(part, axis, [(d, d ^ mask) for d in range(ways)])  21.7 us
    eq x1, other arithmetic, shards(): adjacency = (rowsel[:, None, :] == row_ids).astype(jnp.bfloat16)  9.71 us
    all_to_all x1, starting transfers between devices, shards(): lax.all_to_all(node_features, 'mp', split_axis=1, concat_axis=0, tiled=True)  7.44 us
  transfers between devices with their start and end apart: 19, of which 7 were waited for; matrix products, arithmetic and copies ran while one was open for 15% of the time, Pallas kernels for 0%

profile of v1, /device:TPU:0, one launch (start us, length us, event | category | flops | bytes accessed | tf_op | source)
XLA Modules:
  0.0 319.9 jit_solution(17859688942353271511)
XLA Ops:
  7.2 1.3 all_to_all.26
  9.3 7.4 %all-to-all-start = ((bf16[32,16,192]{2,0,1:T(8,128)(2,1)}), bf16[32,16,192]{2,0,1:T(8,128)(2,1)}, u32[]{:S(2)}, u32[]{:S(2)}) async-start(bf16[32,16,192]{2,0,1:T(8,128)(2,1)} %copy.25), calls=%async_computation | async-start | bytes 524288 | tf_op jit(solution)/shard_map/all_to_all | solution.py:72
  18.1 1.8 select_reduce_fusion
  21.8 2.2 convolution_convert_fusion
  24.1 2.5 copy.28
  26.8 5.8 %all-to-all-start.2 = ((bf16[512,16,144]{0,2,1:T(8,128)(2,1)}), bf16[512,16,144]{0,2,1:T(8,128)(2,1)S(1)}, u32[]{:S(2)}, u32[]{:S(2)}) async-start(bf16[512,16,144]{0,2,1:T(8,128)(2,1)} %bitcast.29), calls=%async_computation.2 | async-start | bytes 4718592 | tf_op jit(solution)/shard_map/all_to_all | solution.py:116
  32.7 9.7 %bitcast_compare_fusion = pred[3072,3072]{1,0:T(32,128)(4,1)} fusion(s32[3072]{0:T(1024)S(1)} %eq.95, s32[16,3072]{1,0:T(8,128)S(1)} %select_reduce_fusion), kind=kLoop, calls=%fused_computation | loop fusion | flops 9437184 | bytes 9646080 | tf_op jit(solution)/shard_map/layer_one_mean/eq | solution.py:63
  42.4 8.5 %fusion = bf16[3072,32]{0,1:T(8,128)(2,1)S(1)} fusion(pred[3072,3072]{1,0:T(32,128)(4,1)} %bitcast_compare_fusion, bf16[32,3072]{1,0:T(8,128)(2,1)S(1)} %copy-done.8, f32[3072]{0:T(1024)S(1)} %convert_divide_fusion), kind=kOutput, calls=%fused_computation.5 | convolution fusion | flops 604176384 | bytes 9842688 | tf_op jit(solution)/shard_map/layer_one_mean/dot_general | solution.py:38
  51.6 1.7 collective-permute-start.1
  53.3 1.7 collective-permute-start.3
  55.9 2.1 fusion.10
  58.1 2.6 collective-permute-start.5
  60.9 2.5 collective-permute-start.7
  63.4 8.8 %collective-permute-done.3 = bf16[32,192]{1,0:T(8,128)(2,1)S(1)} collective-permute-done((bf16[32,192]{1,0:T(8,128)(2,1)S(1)}, bf16[32,192]{1,0:T(8,128)(2,1)S(1)}, u32[]{:S(2)}, u32[]{:S(2)}) %collective-permute-start.3) | collective-permute-done | bytes 12320 | tf_op jit(solution)/shard_map/ppermute | solution.py:18
  72.2 3.5 %collective-permute-start.8 = (bf16[32,192]{1,0:T(8,128)(2,1)S(1)}, bf16[32,192]{1,0:T(8,128)(2,1)S(1)}, u32[]{:S(2)}, u32[]{:S(2)}) collective-permute-start(bf16[32,192]{1,0:T(8,128)(2,1)S(1)} %get-tuple-element.8), channel_id=1, source_target_pairs={{0,9},{1,8},{2,11},{3,10},{4,13},{5,12},{6,15},{7,14},{8,1},{9,0},... | collective-permute-start | bytes 36872 | tf_op jit(solution)/shard_map/ppermute | solution.py:18
  75.7 2.4 collective-permute-start.9
  78.1 2.1 collective-permute-start.10
  80.3 9.5 %collective-permute-done.7 = bf16[32,192]{1,0:T(8,128)(2,1)S(1)} collective-permute-done((bf16[32,192]{1,0:T(8,128)(2,1)S(1)}, bf16[32,192]{1,0:T(8,128)(2,1)S(1)}, u32[]{:S(2)}, u32[]{:S(2)}) %collective-permute-start.7) | collective-permute-done | bytes 12320 | tf_op jit(solution)/shard_map/ppermute | solution.py:18
  89.8 3.2 %collective-permute-start.13 = (bf16[32,192]{1,0:T(8,128)(2,1)S(1)}, bf16[32,192]{1,0:T(8,128)(2,1)S(1)}, u32[]{:S(2)}, u32[]{:S(2)}) collective-permute-start(bf16[32,192]{1,0:T(8,128)(2,1)S(1)} %get-tuple-element.3), channel_id=1, source_target_pairs={{0,14},{1,15},{2,12},{3,13},{4,10},{5,11},{6,8},{7,9},{8,6},{9,7},... | collective-permute-start | bytes 36872 | tf_op jit(solution)/shard_map/ppermute | solution.py:18
  93.1 2.4 collective-permute-start.14
  96.3 2.6 collective-permute-done.14
  98.9 1.4 fusion.32
  100.4 1.3 fusion.17
  101.7 2.4 convolution_convert_fusion.1
  104.1 4.3 %copy.27 = bf16[512,2304]{0,1:T(8,128)(2,1)} copy(bf16[512,2304]{1,0:T(8,128)(2,1)} %convolution_convert_fusion.1) | data formatting | bytes 4718592 | tf_op jit(solution)/shard_map/convert_element_type | solution.py:104
  108.4 4.4 %all-to-all-start.1 = ((bf16[512,16,144]{0,2,1:T(8,128)(2,1)}), bf16[512,16,144]{0,2,1:T(8,128)(2,1)}, u32[]{:S(2)}, u32[]{:S(2)}) async-start(bf16[512,16,144]{0,2,1:T(8,128)(2,1)} %bitcast.25), calls=%async_computation.1 | async-start | bytes 4718592 | tf_op jit(solution)/shard_map/all_to_all | solution.py:105
  112.9 1.4 fusion.41
  114.3 2.0 convolution_bitcast_fusion.1
  118.2 40.3 %all-to-all-done.1 = bf16[512,16,144]{0,2,1:T(8,128)(2,1)} async-done(((bf16[512,16,144]{0,2,1:T(8,128)(2,1)}), bf16[512,16,144]{0,2,1:T(8,128)(2,1)}, u32[]{:S(2)}, u32[]{:S(2)}) %all-to-all-start.1) | async-done | bytes 2359328 | tf_op jit(solution)/shard_map/all_to_all | solution.py:105
  158.5 2.5 fusion.25
  161.4 2.4 pad_maximum_fusion
  166.4 146.6 %reduce-scatter.2.cloned.1.call-done = f32[64,512]{1,0:T(8,128)} async-done(((f32[2048,512]{1,0:T(8,128)}), f32[64,512]{1,0:T(8,128)}) %reduce-scatter.2.cloned.1.call-update) | async-done | bytes 131088 | tf_op jit(solution)/shard_map/reduce_scatter | solution.py:129
  (91 shorter events, 11.8 us)
Async XLA Ops:
  7.2 14.7 %copy-start = (bf16[192,512]{1,0:T(8,128)(2,1)S(1)}, bf16[192,512]{1,0:T(8,128)(2,1)}, u32[]{:S(2)}) copy-start(bf16[192,512]{1,0:T(8,128)(2,1)} %param.13) | copy-start | bytes 589828
  9.3 17.5 %all-to-all-start = ((bf16[32,16,192]{2,0,1:T(8,128)(2,1)}), bf16[32,16,192]{2,0,1:T(8,128)(2,1)}, u32[]{:S(2)}, u32[]{:S(2)}) async-start(bf16[32,16,192]{2,0,1:T(8,128)(2,1)} %copy.25), calls=%async_computation | async-start | bytes 524288 | tf_op jit(solution)/shard_map/all_to_all | solution.py:72
  20.1 0.9 copy-start.1
  20.6 0.7 copy-start.7
  20.8 5.8 %copy-start.9 = (pred[16,1,192]{2,0,1:T(8,128)(4,1)}, pred[16,1,192]{2,0,1:T(8,128)(4,1)S(1)}, u32[]{:S(2)}) copy-start(pred[16,1,192]{2,0,1:T(8,128)(4,1)S(1)} %copy.34) | copy-start | bytes 9220
  21.0 5.6 %copy-start.10 = (f32[192]{0:T(256)}, f32[192]{0:T(256)S(1)}, u32[]{:S(2)}) copy-start(f32[192]{0:T(256)S(1)} %dynamic_slice.91) | copy-start | bytes 2308
  26.8 81.6 %all-to-all-start.2 = ((bf16[512,16,144]{0,2,1:T(8,128)(2,1)}), bf16[512,16,144]{0,2,1:T(8,128)(2,1)S(1)}, u32[]{:S(2)}, u32[]{:S(2)}) async-start(bf16[512,16,144]{0,2,1:T(8,128)(2,1)} %bitcast.29), calls=%async_computation.2 | async-start | bytes 4718592 | tf_op jit(solution)/shard_map/all_to_all | solution.py:116
  32.7 9.7 %copy-start.8 = (bf16[32,3072]{1,0:T(8,128)(2,1)S(1)}, bf16[32,3072]{1,0:T(8,128)(2,1)}, u32[]{:S(2)}) copy-start(bf16[32,3072]{1,0:T(8,128)(2,1)} %param.7) | copy-start | bytes 589828
  51.2 6.9 %collective-permute-start = (bf16[32,192]{1,0:T(8,128)(2,1)S(1)}, bf16[32,192]{1,0:T(8,128)(2,1)S(1)}, u32[]{:S(2)}, u32[]{:S(2)}) collective-permute-start(bf16[32,192]{1,0:T(8,128)(2,1)S(1)} %get-tuple-element.16), channel_id=1, source_target_pairs={{0,1},{1,0},{2,3},{3,2},{4,5},{5,4},{6,7},{7,6},{8,9},{9,8},{10,11... | collective-permute-start | bytes 36872 | tf_op jit(solution)/shard_map/ppermute | solution.py:18
  51.6 9.2 %collective-permute-start.1 = (bf16[32,192]{1,0:T(8,128)(2,1)S(1)}, bf16[32,192]{1,0:T(8,128)(2,1)S(1)}, u32[]{:S(2)}, u32[]{:S(2)}) collective-permute-start(bf16[32,192]{1,0:T(8,128)(2,1)S(1)} %get-tuple-element.15), channel_id=1, source_target_pairs={{0,2},{1,3},{2,0},{3,1},{4,6},{5,7},{6,4},{7,5},{8,10},{9,11},{10,... | collective-permute-start | bytes 36872 | tf_op jit(solution)/shard_map/ppermute | solution.py:18
  53.3 7.6 %collective-permute-start.2 = (bf16[32,192]{1,0:T(8,128)(2,1)S(1)}, bf16[32,192]{1,0:T(8,128)(2,1)S(1)}, u32[]{:S(2)}, u32[]{:S(2)}) collective-permute-start(bf16[32,192]{1,0:T(8,128)(2,1)S(1)} %get-tuple-element.14), channel_id=1, source_target_pairs={{0,3},{1,2},{2,1},{3,0},{4,7},{5,6},{6,5},{7,4},{8,11},{9,10},{10,... | collective-permute-start | bytes 36872 | tf_op jit(solution)/shard_map/ppermute | solution.py:18
  53.3 18.9 %collective-permute-start.3 = (bf16[32,192]{1,0:T(8,128)(2,1)S(1)}, bf16[32,192]{1,0:T(8,128)(2,1)S(1)}, u32[]{:S(2)}, u32[]{:S(2)}) collective-permute-start(bf16[32,192]{1,0:T(8,128)(2,1)S(1)} %get-tuple-element.13), channel_id=1, source_target_pairs={{0,4},{1,5},{2,6},{3,7},{4,0},{5,1},{6,2},{7,3},{8,12},{9,13},{10,... | collective-permute-start | bytes 36872 | tf_op jit(solution)/shard_map/ppermute | solution.py:18
  55.0 20.7 %collective-permute-start.4 = (bf16[32,192]{1,0:T(8,128)(2,1)S(1)}, bf16[32,192]{1,0:T(8,128)(2,1)S(1)}, u32[]{:S(2)}, u32[]{:S(2)}) collective-permute-start(bf16[32,192]{1,0:T(8,128)(2,1)S(1)} %get-tuple-element.12), channel_id=1, source_target_pairs={{0,5},{1,4},{2,7},{3,6},{4,1},{5,0},{6,3},{7,2},{8,13},{9,12},{10,... | collective-permute-start | bytes 36872 | tf_op jit(solution)/shard_map/ppermute | solution.py:18
  58.1 43.6 %copy-start.11 = (bf16[16,144,192]{2,1,0:T(8,128)(2,1)S(1)}, bf16[16,144,192]{2,1,0:T(8,128)(2,1)}, u32[]{:S(2)}) copy-start(bf16[16,144,192]{2,1,0:T(8,128)(2,1)} %fusion.10) | copy-start | bytes 2654212
  58.1 19.9 %collective-permute-start.5 = (bf16[32,192]{1,0:T(8,128)(2,1)S(1)}, bf16[32,192]{1,0:T(8,128)(2,1)S(1)}, u32[]{:S(2)}, u32[]{:S(2)}) collective-permute-start(bf16[32,192]{1,0:T(8,128)(2,1)S(1)} %get-tuple-element.11), channel_id=1, source_target_pairs={{0,6},{1,7},{2,4},{3,5},{4,2},{5,3},{6,0},{7,1},{8,14},{9,15},{10,... | collective-permute-start | bytes 36872 | tf_op jit(solution)/shard_map/ppermute | solution.py:18
  60.8 19.4 %collective-permute-start.6 = (bf16[32,192]{1,0:T(8,128)(2,1)S(1)}, bf16[32,192]{1,0:T(8,128)(2,1)S(1)}, u32[]{:S(2)}, u32[]{:S(2)}) collective-permute-start(bf16[32,192]{1,0:T(8,128)(2,1)S(1)} %get-tuple-element.10), channel_id=1, source_target_pairs={{0,7},{1,6},{2,5},{3,4},{4,3},{5,2},{6,1},{7,0},{8,15},{9,14},{10,... | collective-permute-start | bytes 36872 | tf_op jit(solution)/shard_map/ppermute | solution.py:18
  60.9 29.0 %collective-permute-start.7 = (bf16[32,192]{1,0:T(8,128)(2,1)S(1)}, bf16[32,192]{1,0:T(8,128)(2,1)S(1)}, u32[]{:S(2)}, u32[]{:S(2)}) collective-permute-start(bf16[32,192]{1,0:T(8,128)(2,1)S(1)} %get-tuple-element.9), channel_id=1, source_target_pairs={{0,8},{1,9},{2,10},{3,11},{4,12},{5,13},{6,14},{7,15},{8,0},{9,1},... | collective-permute-start | bytes 36872 | tf_op jit(solution)/shard_map/ppermute | solution.py:18
  72.2 17.6 %collective-permute-start.8 = (bf16[32,192]{1,0:T(8,128)(2,1)S(1)}, bf16[32,192]{1,0:T(8,128)(2,1)S(1)}, u32[]{:S(2)}, u32[]{:S(2)}) collective-permute-start(bf16[32,192]{1,0:T(8,128)(2,1)S(1)} %get-tuple-element.8), channel_id=1, source_target_pairs={{0,9},{1,8},{2,11},{3,10},{4,13},{5,12},{6,15},{7,14},{8,1},{9,0},... | collective-permute-start | bytes 36872 | tf_op jit(solution)/shard_map/ppermute | solution.py:18
  75.7 17.4 %collective-permute-start.9 = (bf16[32,192]{1,0:T(8,128)(2,1)S(1)}, bf16[32,192]{1,0:T(8,128)(2,1)S(1)}, u32[]{:S(2)}, u32[]{:S(2)}) collective-permute-start(bf16[32,192]{1,0:T(8,128)(2,1)S(1)} %get-tuple-element.7), channel_id=1, source_target_pairs={{0,10},{1,11},{2,8},{3,9},{4,14},{5,15},{6,12},{7,13},{8,2},{9,3},... | collective-permute-start | bytes 36872 | tf_op jit(solution)/shard_map/ppermute | solution.py:18
  78.1 17.4 %collective-permute-start.10 = (bf16[32,192]{1,0:T(8,128)(2,1)S(1)}, bf16[32,192]{1,0:T(8,128)(2,1)S(1)}, u32[]{:S(2)}, u32[]{:S(2)}) collective-permute-start(bf16[32,192]{1,0:T(8,128)(2,1)S(1)} %get-tuple-element.6), channel_id=1, source_target_pairs={{0,11},{1,10},{2,9},{3,8},{4,15},{5,14},{6,13},{7,12},{8,3},{9,2},... | collective-permute-start | bytes 36872 | tf_op jit(solution)/shard_map/ppermute | solution.py:18
  80.2 15.2 %collective-permute-start.11 = (bf16[32,192]{1,0:T(8,128)(2,1)S(1)}, bf16[32,192]{1,0:T(8,128)(2,1)S(1)}, u32[]{:S(2)}, u32[]{:S(2)}) collective-permute-start(bf16[32,192]{1,0:T(8,128)(2,1)S(1)} %get-tuple-element.5), channel_id=1, source_target_pairs={{0,12},{1,13},{2,14},{3,15},{4,8},{5,9},{6,10},{7,11},{8,4},{9,5},... | collective-permute-start | bytes 36872 | tf_op jit(solution)/shard_map/ppermute | solution.py:18
  89.8 5.7 %collective-permute-start.12 = (bf16[32,192]{1,0:T(8,128)(2,1)S(1)}, bf16[32,192]{1,0:T(8,128)(2,1)S(1)}, u32[]{:S(2)}, u32[]{:S(2)}) collective-permute-start(bf16[32,192]{1,0:T(8,128)(2,1)S(1)} %get-tuple-element.4), channel_id=1, source_target_pairs={{0,13},{1,12},{2,15},{3,14},{4,9},{5,8},{6,11},{7,10},{8,5},{9,4},... | collective-permute-start | bytes 36872 | tf_op jit(solution)/shard_map/ppermute | solution.py:18
  89.8 6.5 %collective-permute-start.13 = (bf16[32,192]{1,0:T(8,128)(2,1)S(1)}, bf16[32,192]{1,0:T(8,128)(2,1)S(1)}, u32[]{:S(2)}, u32[]{:S(2)}) collective-permute-start(bf16[32,192]{1,0:T(8,128)(2,1)S(1)} %get-tuple-element.3), channel_id=1, source_target_pairs={{0,14},{1,15},{2,12},{3,13},{4,10},{5,11},{6,8},{7,9},{8,6},{9,7},... | collective-permute-start | bytes 36872 | tf_op jit(solution)/shard_map/ppermute | solution.py:18
  93.1 5.9 %collective-permute-start.14 = (bf16[32,192]{1,0:T(8,128)(2,1)S(1)}, bf16[32,192]{1,0:T(8,128)(2,1)S(1)}, u32[]{:S(2)}, u32[]{:S(2)}) collective-permute-start(bf16[32,192]{1,0:T(8,128)(2,1)S(1)} %get-tuple-element.2), channel_id=1, source_target_pairs={{0,15},{1,14},{2,13},{3,12},{4,11},{5,10},{6,9},{7,8},{8,7},{9,6},... | collective-permute-start | bytes 36872 | tf_op jit(solution)/shard_map/ppermute | solution.py:18
  101.7 14.6 %copy-start.5 = (f32[512,192]{0,1:T(8,128)}, f32[512,192]{0,1:T(8,128)S(1)}, u32[]{:S(2)}) copy-start(f32[512,192]{0,1:T(8,128)S(1)} %fusion.17) | copy-start | bytes 1179652
  108.4 50.1 %all-to-all-start.1 = ((bf16[512,16,144]{0,2,1:T(8,128)(2,1)}), bf16[512,16,144]{0,2,1:T(8,128)(2,1)}, u32[]{:S(2)}, u32[]{:S(2)}) async-start(bf16[512,16,144]{0,2,1:T(8,128)(2,1)} %bitcast.25), calls=%async_computation.1 | async-start | bytes 4718592 | tf_op jit(solution)/shard_map/all_to_all | solution.py:105
  112.9 200.1 %reduce-scatter.2.cloned.1.call-start = ((), (), s32[]{:S(2)}) async-start(), calls=%async_computation.4 | async-start | bytes 4325376 | tf_op jit(solution)/shard_map/reduce_scatter | solution.py:129
  114.3 2.0 copy-start.2
  118.2 43.2 %copy-start.4 = (f32[512,512]{1,0:T(8,128)S(1)}, f32[512,512]{1,0:T(8,128)}, u32[]{:S(2)}) copy-start(f32[512,512]{1,0:T(8,128)} %fusion.41) | copy-start | bytes 3145732
  163.8 1.2 copy-start.3
  163.8 1.3 copy-start.6
Sparse Core Ops, SparseCore 0:
  164.0 148.9 reduce-scatter.1
